TPU v7x, 512 devices: a whole 4x4x16 slice. The times are simulated.
512 devices in a mesh: node: 8 (over y, x_lo), space: 64 (over z, x_hi, core).
Axes of the slice: x: 4 (x_hi: 2, x_lo: 2; x = x_hi * 2 + x_lo), y: 4, z: 16, core: 2. Of those that a mesh axis runs over, the one named last changes fastest.
Arguments:
- grain_ids: int32 [256, 16, 128], P('space'), may hold values from 0 to 7
- peak_heat: float32 [256, 16, 128], P('space'), may hold values from 0.5 to 1
Outputs:
- node_states: float32 [8, 8, 256, 16, 128], P('node', None, 'space')
All inputs are finite; a program needn't handle non-finite values.
Results may differ from a plain program's by a relative error of at most 0.0001.
Values sent between devices are 32-bit elements; how exact they have to be, the bound alone decides.
No kernel may reach another device: no remote copies, remote signals or barrier semaphores. Data moves between devices by JAX's collectives and lax.ppermute only.
A program may use at most 64 MiB of HBM per device.

v0:
```python
import math
import jax
import jax.numpy as jnp
import numpy as np
from jax import lax
from jax.sharding import PartitionSpec as P

P_SIZE = 8
NODE_DEV = 1
SWEEPS = 3
JACOBI = 2
STEPS = 2
time_step = 0.25
cross_coef = 1.5
base_heat = 0.45
activation = 3.0


def with_halo(block, sides, width):
    for axis, dim in sides:
        count = lax.axis_size(axis)
        forward = [(i, i + 1) for i in range(count - 1)]
        forward.append((count - 1, 0))
        backward = [(target, source) for source, target in forward]
        low = lax.ppermute(
            lax.slice_in_dim(block, block.shape[dim] - width, None, axis=dim), axis, forward
        )
        high = lax.ppermute(lax.slice_in_dim(block, 0, width, axis=dim), axis, backward)
        block = jnp.concatenate([low, block, high], axis=dim)
    return block


def broadcast(block, axis, source):
    block = jnp.where(lax.axis_index(axis) == source, block, jnp.zeros_like(block))
    return lax.psum(block, axis)


def legendre_pair(count, point):
    before = 1.0
    current = point
    for degree in range(2, count + 1):
        following = ((2 * degree - 1) * point * current - (degree - 1) * before) / degree
        before = current
        current = following
    return (current, before)


def radau_value(count, point):
    high, low = legendre_pair(count, point)
    high_prev, low_prev = legendre_pair(count - 1, point)
    value = high - low
    slope_high = count * (point * high - low) / (point * point - 1.0)
    slope_low = (count - 1) * (point * high_prev - low_prev) / (point * point - 1.0)
    return (value, slope_high - slope_low)


def radau_table(count):
    roots = [1.0]
    for index in range(1, count):
        point = math.cos(2.0 * math.pi * index / (2 * count - 1))
        for repeat in range(100):
            value, slope = radau_value(count, point)
            point = point - value / slope
        roots.append(point)
    roots = sorted(roots)
    times_list = [(value + 1.0) / 2.0 for value in roots]
    times_list[-1] = 1.0
    table = []
    for row_index in range(count):
        upper = times_list[row_index]
        row_values = []
        for column in range(count):
            poly = [1.0]
            for other in range(count):
                if other != column:
                    scale = times_list[column] - times_list[other]
                    shifted = [0.0] + poly
                    scaled = [c * times_list[other] for c in poly] + [0.0]
                    poly = [(shifted[i] - scaled[i]) / scale for i in range(len(shifted))]
            integral_value = 0.0
            for power in range(len(poly)):
                integral_value += poly[power] * upper ** (power + 1) / (power + 1)
            row_values.append(integral_value)
        table.append(row_values)
    return (np.array(times_list), np.array(table))


def drive(field):
    squares = field * field
    total = jnp.sum(squares, axis=-4, keepdims=True)
    return -field + squares * field + 2.0 * cross_coef * field * (total - squares)


def near_sum(extended):
    inner = extended[..., 1:-1, :, :]
    result = extended[..., 2:, :, :] + extended[..., :-2, :, :]
    result = result + jnp.roll(inner, -1, -2) + jnp.roll(inner, 1, -2)
    return result + jnp.roll(inner, -1, -1) + jnp.roll(inner, 1, -1)


def heat_mobility(peak, moment):
    middle = 0.5 * time_step * STEPS
    theta = base_heat + (peak - base_heat) * jnp.exp(-(((moment - middle) / middle) ** 2))
    return jnp.exp(activation * (1.0 - 1.0 / theta))


def rate_on(extended, mobility):
    inner = extended[..., 1:-1, :, :]
    return -mobility * (drive(inner) - (near_sum(extended) - 6.0 * inner))


def relax_on(extended, goal, factor):
    inner = extended[..., 1:-1, :, :]
    return (goal + factor * (near_sum(extended) - drive(inner))) / (1.0 + 6.0 * factor)


def on_device(grain_ids, peak_heat):
    total_nodes = lax.axis_size("node") * NODE_DEV
    node_times, table = radau_table(total_nodes)
    weights = jnp.asarray(table, jnp.float32)
    first = lax.axis_index("node") * NODE_DEV
    times = lax.dynamic_slice_in_dim(jnp.asarray(node_times, jnp.float32), first, NODE_DEV, 0)
    my_rows = lax.dynamic_slice_in_dim(weights, first, NODE_DEV, 0)
    taus = times.reshape((NODE_DEV, 1, 1, 1, 1))
    orders = jnp.arange(P_SIZE, dtype=jnp.int32)
    start = (grain_ids[None] == orders[:, None, None, None]).astype(jnp.float32)
    states = None
    for step_index in range(STEPS):
        moments = (step_index + times) * time_step
        mobility = heat_mobility(peak_heat[None], moments[:, None, None, None])[:, None]
        factor = time_step * taus * mobility
        start_wide = with_halo(start, (("space", 1),), 1)
        rates = rate_on(start_wide[None], mobility)
        states = jnp.broadcast_to(start[None], rates.shape)
        for sweep_index in range(SWEEPS):
            piece = lax.all_gather(rates, "node", axis=0, tiled=True)
            coefs = lax.slice_in_dim(my_rows, 0, piece.shape[0], axis=1)
            quad = jnp.zeros_like(rates) + jnp.tensordot(
                coefs, piece, axes=1, precision=lax.Precision.HIGHEST
            )
            goal = start[None] + time_step * quad - time_step * taus * rates
            last = sweep_index + 1 == SWEEPS
            passes = JACOBI if last else JACOBI + 1
            for relax_index in range(passes):
                extended = with_halo(states, (("space", 2),), 1)
                if relax_index < JACOBI:
                    states = relax_on(extended, goal, factor)
                else:
                    rates = rate_on(extended, mobility)
        if step_index + 1 < STEPS:
            start = broadcast(states[-1], "node", lax.axis_size("node") - 1)
    return states


def solution(mesh):
    in_specs = (P("space", None, None), P("space", None, None))
    out_specs = P("node", None, "space", None, None)
    return jax.shard_map(
        on_device, mesh=mesh, in_specs=in_specs, out_specs=out_specs, check_vma=False
    )
```

profile of v0, /device:TPU:8, one launch (start us, length us, event | category | flops | bytes accessed | tf_op | source)
XLA Modules:
  0.0 647.7 jit_solution(4075357415516616793)
XLA Ops:
  7.3 1.9 collective-permute-start
  9.3 13.3 %collective-permute-start.1 = (f32[8,1,16,128]{3,2,1,0:T(8,128)S(1)}, f32[8,1,16,128]{3,2,1,0:T(8,128)S(1)}, u32[]{:S(2)}, u32[]{:S(2)}) collective-permute-start(f32[8,1,16,128]{3,2,1,0:T(8,128)S(1)} %get-tuple-element.166), channel_id=1, source_target_pairs={{1,0},{2,1},{3,2},{4,3},{5,4},{6,5},{7,6},{8,7},{9,8},{10,9},{11,1... | collective-permute-start | bytes 196616 | tf_op jit(solution)/shard_map/ppermute | solution.py:28
  27.6 5.7 collective-permute-start.2
  33.3 1.9 collective-permute-start.3
  35.7 47.7 %all-gather.7.cloned.1.call-done = f32[8,8,4,16,128]{4,3,2,1,0:T(8,128)} async-done(((f32[1,8,4,16,128]{4,3,2,1,0:T(8,128)}), f32[8,8,4,16,128]{4,3,2,1,0:T(8,128)}) %all-gather.7.cloned.1.call-update) | async-done | bytes 2097168 | tf_op jit(solution)/shard_map/all_gather | solution.py:136
  83.4 4.4 fusion.10
  88.6 7.5 %collective-permute-start.4 = (f32[1,8,1,16,128]{4,3,2,1,0:T(8,128)S(1)}, f32[1,8,1,16,128]{4,3,2,1,0:T(8,128)S(1)}, u32[]{:S(2)}, u32[]{:S(2)}) collective-permute-start(f32[1,8,1,16,128]{4,3,2,1,0:T(8,128)S(1)} %get-tuple-element.155), channel_id=1, source_target_pairs={{1,0},{2,1},{3,2},{4,3},{5,4},{6,5},{7,6},{8,7},{9,8},{10,9},{11,1... | collective-permute-start | bytes 196616 | tf_op jit(solution)/shard_map/ppermute | solution.py:28
  96.1 1.9 collective-permute-start.5
  98.1 7.2 %collective-permute-done.5 = f32[1,8,1,16,128]{4,3,2,1,0:T(8,128)S(1)} collective-permute-done((f32[1,8,1,16,128]{4,3,2,1,0:T(8,128)S(1)}, f32[1,8,1,16,128]{4,3,2,1,0:T(8,128)S(1)}, u32[]{:S(2)}, u32[]{:S(2)}) %collective-permute-start.5) | collective-permute-done | bytes 65568 | tf_op jit(solution)/shard_map/ppermute | solution.py:25
  106.0 1.9 collective-permute-start.6
  108.0 2.4 collective-permute-start.7
  110.4 6.7 %collective-permute-done.7 = f32[1,8,1,16,128]{4,3,2,1,0:T(8,128)S(1)} collective-permute-done((f32[1,8,1,16,128]{4,3,2,1,0:T(8,128)S(1)}, f32[1,8,1,16,128]{4,3,2,1,0:T(8,128)S(1)}, u32[]{:S(2)}, u32[]{:S(2)}) %collective-permute-start.7) | collective-permute-done | bytes 65568 | tf_op jit(solution)/shard_map/ppermute | solution.py:25
  118.2 53.8 %all-gather.9.cloned.1.call-done = f32[8,8,4,16,128]{4,3,2,1,0:T(8,128)} async-done(((f32[1,8,4,16,128]{4,3,2,1,0:T(8,128)}), f32[8,8,4,16,128]{4,3,2,1,0:T(8,128)}) %all-gather.9.cloned.1.call-update) | async-done | bytes 2097168 | tf_op jit(solution)/shard_map/all_gather | solution.py:136
  172.1 4.4 fusion.8
  177.1 7.5 %collective-permute-start.8 = (f32[1,8,1,16,128]{4,3,2,1,0:T(8,128)S(1)}, f32[1,8,1,16,128]{4,3,2,1,0:T(8,128)S(1)}, u32[]{:S(2)}, u32[]{:S(2)}) collective-permute-start(f32[1,8,1,16,128]{4,3,2,1,0:T(8,128)S(1)} %get-tuple-element.135), channel_id=1, source_target_pairs={{1,0},{2,1},{3,2},{4,3},{5,4},{6,5},{7,6},{8,7},{9,8},{10,9},{11,1... | collective-permute-start | bytes 196616 | tf_op jit(solution)/shard_map/ppermute | solution.py:28
  184.6 1.9 collective-permute-start.9
  186.5 7.2 %collective-permute-done.9 = f32[1,8,1,16,128]{4,3,2,1,0:T(8,128)S(1)} collective-permute-done((f32[1,8,1,16,128]{4,3,2,1,0:T(8,128)S(1)}, f32[1,8,1,16,128]{4,3,2,1,0:T(8,128)S(1)}, u32[]{:S(2)}, u32[]{:S(2)}) %collective-permute-start.9) | collective-permute-done | bytes 65568 | tf_op jit(solution)/shard_map/ppermute | solution.py:25
  194.5 1.9 collective-permute-start.10
  196.4 2.4 collective-permute-start.11
  198.9 6.7 %collective-permute-done.11 = f32[1,8,1,16,128]{4,3,2,1,0:T(8,128)S(1)} collective-permute-done((f32[1,8,1,16,128]{4,3,2,1,0:T(8,128)S(1)}, f32[1,8,1,16,128]{4,3,2,1,0:T(8,128)S(1)}, u32[]{:S(2)}, u32[]{:S(2)}) %collective-permute-start.11) | collective-permute-done | bytes 65568 | tf_op jit(solution)/shard_map/ppermute | solution.py:25
  206.9 53.6 %all-gather.11.cloned.1.call-done = f32[8,8,4,16,128]{4,3,2,1,0:T(8,128)} async-done(((f32[1,8,4,16,128]{4,3,2,1,0:T(8,128)}), f32[8,8,4,16,128]{4,3,2,1,0:T(8,128)}) %all-gather.11.cloned.1.call-update) | async-done | bytes 2097168 | tf_op jit(solution)/shard_map/all_gather | solution.py:136
  260.5 4.4 fusion.6
  265.5 7.5 %collective-permute-start.12 = (f32[1,8,1,16,128]{4,3,2,1,0:T(8,128)S(1)}, f32[1,8,1,16,128]{4,3,2,1,0:T(8,128)S(1)}, u32[]{:S(2)}, u32[]{:S(2)}) collective-permute-start(f32[1,8,1,16,128]{4,3,2,1,0:T(8,128)S(1)} %get-tuple-element.115), channel_id=1, source_target_pairs={{1,0},{2,1},{3,2},{4,3},{5,4},{6,5},{7,6},{8,7},{9,8},{10,9},{11,1... | collective-permute-start | bytes 196616 | tf_op jit(solution)/shard_map/ppermute | solution.py:28
  273.0 1.9 collective-permute-start.13
  275.0 7.2 %collective-permute-done.13 = f32[1,8,1,16,128]{4,3,2,1,0:T(8,128)S(1)} collective-permute-done((f32[1,8,1,16,128]{4,3,2,1,0:T(8,128)S(1)}, f32[1,8,1,16,128]{4,3,2,1,0:T(8,128)S(1)}, u32[]{:S(2)}, u32[]{:S(2)}) %collective-permute-start.13) | collective-permute-done | bytes 65568 | tf_op jit(solution)/shard_map/ppermute | solution.py:25
  283.4 83.6 %all-reduce.2.cloned.1.call-done = f32[8,4,16,128]{3,2,1,0:T(8,128)} async-done(((f32[8,4,16,128]{3,2,1,0:T(8,128)}), f32[8,4,16,128]{3,2,1,0:T(8,128)}) %all-reduce.2.cloned.1.call-update) | async-done | bytes 262160 | tf_op jit(solution)/shard_map/psum | solution.py:35
  367.9 1.9 collective-permute-start.14
  369.8 7.3 %collective-permute-start.15 = (f32[8,1,16,128]{3,2,1,0:T(8,128)S(1)}, f32[8,1,16,128]{3,2,1,0:T(8,128)S(1)}, u32[]{:S(2)}, u32[]{:S(2)}) collective-permute-start(f32[8,1,16,128]{3,2,1,0:T(8,128)S(1)} %get-tuple-element.104), channel_id=1, source_target_pairs={{1,0},{2,1},{3,2},{4,3},{5,4},{6,5},{7,6},{8,7},{9,8},{10,9},{11,1... | collective-permute-start | bytes 196616 | tf_op jit(solution)/shard_map/ppermute | solution.py:28
  381.5 7.3 %collective-permute-start.16 = (f32[1,8,1,16,128]{4,3,2,1,0:T(8,128)S(1)}, f32[1,8,1,16,128]{4,3,2,1,0:T(8,128)S(1)}, u32[]{:S(2)}, u32[]{:S(2)}) collective-permute-start(f32[1,8,1,16,128]{4,3,2,1,0:T(8,128)S(1)} %get-tuple-element.105), channel_id=1, source_target_pairs={{1,0},{2,1},{3,2},{4,3},{5,4},{6,5},{7,6},{8,7},{9,8},{10,9},{11,1... | collective-permute-start | bytes 196616 | tf_op jit(solution)/shard_map/ppermute | solution.py:28
  388.8 1.9 collective-permute-start.17
  391.1 49.9 %all-gather.13.cloned.1.call-done = f32[8,8,4,16,128]{4,3,2,1,0:T(8,128)} async-done(((f32[1,8,4,16,128]{4,3,2,1,0:T(8,128)}), f32[8,8,4,16,128]{4,3,2,1,0:T(8,128)}) %all-gather.13.cloned.1.call-update) | async-done | bytes 2097168 | tf_op jit(solution)/shard_map/all_gather | solution.py:136
  441.0 4.4 fusion.4
  446.2 7.5 %collective-permute-start.18 = (f32[1,8,1,16,128]{4,3,2,1,0:T(8,128)S(1)}, f32[1,8,1,16,128]{4,3,2,1,0:T(8,128)S(1)}, u32[]{:S(2)}, u32[]{:S(2)}) collective-permute-start(f32[1,8,1,16,128]{4,3,2,1,0:T(8,128)S(1)} %get-tuple-element.93), channel_id=1, source_target_pairs={{1,0},{2,1},{3,2},{4,3},{5,4},{6,5},{7,6},{8,7},{9,8},{10,9},{11,1... | collective-permute-start | bytes 196616 | tf_op jit(solution)/shard_map/ppermute | solution.py:28
  453.7 1.9 collective-permute-start.19
  455.7 7.2 %collective-permute-done.19 = f32[1,8,1,16,128]{4,3,2,1,0:T(8,128)S(1)} collective-permute-done((f32[1,8,1,16,128]{4,3,2,1,0:T(8,128)S(1)}, f32[1,8,1,16,128]{4,3,2,1,0:T(8,128)S(1)}, u32[]{:S(2)}, u32[]{:S(2)}) %collective-permute-start.19) | collective-permute-done | bytes 65568 | tf_op jit(solution)/shard_map/ppermute | solution.py:25
  465.5 2.4 collective-permute-start.21
  468.0 6.7 %collective-permute-done.21 = f32[1,8,1,16,128]{4,3,2,1,0:T(8,128)S(1)} collective-permute-done((f32[1,8,1,16,128]{4,3,2,1,0:T(8,128)S(1)}, f32[1,8,1,16,128]{4,3,2,1,0:T(8,128)S(1)}, u32[]{:S(2)}, u32[]{:S(2)}) %collective-permute-start.21) | collective-permute-done | bytes 65568 | tf_op jit(solution)/shard_map/ppermute | solution.py:25
  476.0 53.6 %all-gather.15.cloned.1.call-done = f32[8,8,4,16,128]{4,3,2,1,0:T(8,128)} async-done(((f32[1,8,4,16,128]{4,3,2,1,0:T(8,128)}), f32[8,8,4,16,128]{4,3,2,1,0:T(8,128)}) %all-gather.15.cloned.1.call-update) | async-done | bytes 2097168 | tf_op jit(solution)/shard_map/all_gather | solution.py:136
  529.6 4.4 fusion.2
  534.6 7.5 %collective-permute-start.22 = (f32[1,8,1,16,128]{4,3,2,1,0:T(8,128)S(1)}, f32[1,8,1,16,128]{4,3,2,1,0:T(8,128)S(1)}, u32[]{:S(2)}, u32[]{:S(2)}) collective-permute-start(f32[1,8,1,16,128]{4,3,2,1,0:T(8,128)S(1)} %get-tuple-element.73), channel_id=1, source_target_pairs={{1,0},{2,1},{3,2},{4,3},{5,4},{6,5},{7,6},{8,7},{9,8},{10,9},{11,1... | collective-permute-start | bytes 196616 | tf_op jit(solution)/shard_map/ppermute | solution.py:28
  542.1 1.9 collective-permute-start.23
  544.1 7.2 %collective-permute-done.23 = f32[1,8,1,16,128]{4,3,2,1,0:T(8,128)S(1)} collective-permute-done((f32[1,8,1,16,128]{4,3,2,1,0:T(8,128)S(1)}, f32[1,8,1,16,128]{4,3,2,1,0:T(8,128)S(1)}, u32[]{:S(2)}, u32[]{:S(2)}) %collective-permute-start.23) | collective-permute-done | bytes 65568 | tf_op jit(solution)/shard_map/ppermute | solution.py:25
  554.0 2.4 collective-permute-start.25
  556.4 6.7 %collective-permute-done.25 = f32[1,8,1,16,128]{4,3,2,1,0:T(8,128)S(1)} collective-permute-done((f32[1,8,1,16,128]{4,3,2,1,0:T(8,128)S(1)}, f32[1,8,1,16,128]{4,3,2,1,0:T(8,128)S(1)}, u32[]{:S(2)}, u32[]{:S(2)}) %collective-permute-start.25) | collective-permute-done | bytes 65568 | tf_op jit(solution)/shard_map/ppermute | solution.py:25
  564.2 53.9 %all-gather.17.cloned.1.call-done = f32[8,8,4,16,128]{4,3,2,1,0:T(8,128)} async-done(((f32[1,8,4,16,128]{4,3,2,1,0:T(8,128)}), f32[8,8,4,16,128]{4,3,2,1,0:T(8,128)}) %all-gather.17.cloned.1.call-update) | async-done | bytes 2097168 | tf_op jit(solution)/shard_map/all_gather | solution.py:136
  618.1 4.4 fusion
  623.1 7.5 %collective-permute-start.26 = (f32[1,8,1,16,128]{4,3,2,1,0:T(8,128)S(1)}, f32[1,8,1,16,128]{4,3,2,1,0:T(8,128)S(1)}, u32[]{:S(2)}, u32[]{:S(2)}) collective-permute-start(f32[1,8,1,16,128]{4,3,2,1,0:T(8,128)S(1)} %get-tuple-element.61), channel_id=1, source_target_pairs={{1,0},{2,1},{3,2},{4,3},{5,4},{6,5},{7,6},{8,7},{9,8},{10,9},{11,1... | collective-permute-start | bytes 196616 | tf_op jit(solution)/shard_map/ppermute | solution.py:28
  632.6 7.2 %collective-permute-done.27 = f32[1,8,1,16,128]{4,3,2,1,0:T(8,128)S(1)} collective-permute-done((f32[1,8,1,16,128]{4,3,2,1,0:T(8,128)S(1)}, f32[1,8,1,16,128]{4,3,2,1,0:T(8,128)S(1)}, u32[]{:S(2)}, u32[]{:S(2)}) %collective-permute-start.27) | collective-permute-done | bytes 65568 | tf_op jit(solution)/shard_map/ppermute | solution.py:25
  (151 shorter events, 29.2 us)
Async XLA Ops:
  6.5 76.9 %all-gather.7.cloned.1.call-start = ((), (), s32[]{:S(2)}) async-start(), calls=%async_computation | async-start | bytes 2359296 | tf_op jit(solution)/shard_map/all_gather | solution.py:136
  7.3 18.7 %collective-permute-start = (f32[8,1,16,128]{3,2,1,0:T(8,128)S(1)}, f32[8,1,16,128]{3,2,1,0:T(8,128)S(1)}, u32[]{:S(2)}, u32[]{:S(2)}) collective-permute-start(f32[8,1,16,128]{3,2,1,0:T(8,128)S(1)} %get-tuple-element.165), channel_id=1, source_target_pairs={{0,1},{1,2},{2,3},{3,4},{4,5},{5,6},{6,7},{7,8},{8,9},{9,10},{10,1... | collective-permute-start | bytes 196616 | tf_op jit(solution)/shard_map/ppermute | solution.py:25
  9.3 16.8 %collective-permute-start.1 = (f32[8,1,16,128]{3,2,1,0:T(8,128)S(1)}, f32[8,1,16,128]{3,2,1,0:T(8,128)S(1)}, u32[]{:S(2)}, u32[]{:S(2)}) collective-permute-start(f32[8,1,16,128]{3,2,1,0:T(8,128)S(1)} %get-tuple-element.166), channel_id=1, source_target_pairs={{1,0},{2,1},{3,2},{4,3},{5,4},{6,5},{7,6},{8,7},{9,8},{10,9},{11,1... | collective-permute-start | bytes 196616 | tf_op jit(solution)/shard_map/ppermute | solution.py:28
  26.3 1.2 copy-start.7
  27.5 55.9 %copy-start.8 = (f32[8,8]{1,0:T(8,128)S(1)}, f32[8,8]{1,0:T(8,128)}, u32[]{:S(2)}) copy-start(f32[8,8]{1,0:T(8,128)} %constant.57.clone) | copy-start | bytes 772
  27.5 144.6 %all-gather.9.cloned.1.call-start = ((), (), s32[]{:S(2)}) async-start(), calls=%async_computation.1 | async-start | bytes 2359296 | tf_op jit(solution)/shard_map/all_gather | solution.py:136
  27.6 60.3 %collective-permute-start.2 = (f32[1,8,1,16,128]{4,3,2,1,0:T(8,128)S(1)}, f32[1,8,1,16,128]{4,3,2,1,0:T(8,128)S(1)}, u32[]{:S(2)}, u32[]{:S(2)}) collective-permute-start(f32[1,8,1,16,128]{4,3,2,1,0:T(8,128)S(1)} %get-tuple-element.167), channel_id=1, source_target_pairs={{1,0},{2,1},{3,2},{4,3},{5,4},{6,5},{7,6},{8,7},{9,8},{10,9},{11,1... | collective-permute-start | bytes 196616 | tf_op jit(solution)/shard_map/ppermute | solution.py:28
  33.3 54.5 %collective-permute-start.3 = (f32[1,8,1,16,128]{4,3,2,1,0:T(8,128)S(1)}, f32[1,8,1,16,128]{4,3,2,1,0:T(8,128)S(1)}, u32[]{:S(2)}, u32[]{:S(2)}) collective-permute-start(f32[1,8,1,16,128]{4,3,2,1,0:T(8,128)S(1)} %get-tuple-element.168), channel_id=1, source_target_pairs={{0,1},{1,2},{2,3},{3,4},{4,5},{5,6},{6,7},{7,8},{8,9},{9,10},{10,1... | collective-permute-start | bytes 196616 | tf_op jit(solution)/shard_map/ppermute | solution.py:25
  35.4 52.5 %copy-start.2 = (f32[1,8,4,16,128]{4,3,2,1,0:T(8,128)S(1)}, f32[1,8,4,16,128]{4,3,2,1,0:T(8,128)}, u32[]{:S(2)}) copy-start(f32[1,8,4,16,128]{4,3,2,1,0:T(8,128)} %fusion.21) | copy-start | bytes 786436
  88.6 9.5 %collective-permute-start.4 = (f32[1,8,1,16,128]{4,3,2,1,0:T(8,128)S(1)}, f32[1,8,1,16,128]{4,3,2,1,0:T(8,128)S(1)}, u32[]{:S(2)}, u32[]{:S(2)}) collective-permute-start(f32[1,8,1,16,128]{4,3,2,1,0:T(8,128)S(1)} %get-tuple-element.155), channel_id=1, source_target_pairs={{1,0},{2,1},{3,2},{4,3},{5,4},{6,5},{7,6},{8,7},{9,8},{10,9},{11,1... | collective-permute-start | bytes 196616 | tf_op jit(solution)/shard_map/ppermute | solution.py:28
  96.1 9.2 %collective-permute-start.5 = (f32[1,8,1,16,128]{4,3,2,1,0:T(8,128)S(1)}, f32[1,8,1,16,128]{4,3,2,1,0:T(8,128)S(1)}, u32[]{:S(2)}, u32[]{:S(2)}) collective-permute-start(f32[1,8,1,16,128]{4,3,2,1,0:T(8,128)S(1)} %get-tuple-element.156), channel_id=1, source_target_pairs={{0,1},{1,2},{2,3},{3,4},{4,5},{5,6},{6,7},{7,8},{8,9},{9,10},{10,1... | collective-permute-start | bytes 196616 | tf_op jit(solution)/shard_map/ppermute | solution.py:25
  106.0 4.4 collective-permute-start.6
  108.0 9.2 %collective-permute-start.7 = (f32[1,8,1,16,128]{4,3,2,1,0:T(8,128)S(1)}, f32[1,8,1,16,128]{4,3,2,1,0:T(8,128)S(1)}, u32[]{:S(2)}, u32[]{:S(2)}) collective-permute-start(f32[1,8,1,16,128]{4,3,2,1,0:T(8,128)S(1)} %get-tuple-element.146), channel_id=1, source_target_pairs={{0,1},{1,2},{2,3},{3,4},{4,5},{5,6},{6,7},{7,8},{8,9},{9,10},{10,1... | collective-permute-start | bytes 196616 | tf_op jit(solution)/shard_map/ppermute | solution.py:25
  118.2 58.3 %copy-start.1 = (f32[1,8,4,16,128]{4,3,2,1,0:T(8,128)S(1)}, f32[1,8,4,16,128]{4,3,2,1,0:T(8,128)}, u32[]{:S(2)}) copy-start(f32[1,8,4,16,128]{4,3,2,1,0:T(8,128)} %get-tuple-element.29) | copy-start | bytes 786436
  118.2 142.3 %all-gather.11.cloned.1.call-start = ((), (), s32[]{:S(2)}) async-start(), calls=%async_computation.2 | async-start | bytes 2359296 | tf_op jit(solution)/shard_map/all_gather | solution.py:136
  177.1 9.5 %collective-permute-start.8 = (f32[1,8,1,16,128]{4,3,2,1,0:T(8,128)S(1)}, f32[1,8,1,16,128]{4,3,2,1,0:T(8,128)S(1)}, u32[]{:S(2)}, u32[]{:S(2)}) collective-permute-start(f32[1,8,1,16,128]{4,3,2,1,0:T(8,128)S(1)} %get-tuple-element.135), channel_id=1, source_target_pairs={{1,0},{2,1},{3,2},{4,3},{5,4},{6,5},{7,6},{8,7},{9,8},{10,9},{11,1... | collective-permute-start | bytes 196616 | tf_op jit(solution)/shard_map/ppermute | solution.py:28
  184.6 9.2 %collective-permute-start.9 = (f32[1,8,1,16,128]{4,3,2,1,0:T(8,128)S(1)}, f32[1,8,1,16,128]{4,3,2,1,0:T(8,128)S(1)}, u32[]{:S(2)}, u32[]{:S(2)}) collective-permute-start(f32[1,8,1,16,128]{4,3,2,1,0:T(8,128)S(1)} %get-tuple-element.136), channel_id=1, source_target_pairs={{0,1},{1,2},{2,3},{3,4},{4,5},{5,6},{6,7},{7,8},{8,9},{9,10},{10,1... | collective-permute-start | bytes 196616 | tf_op jit(solution)/shard_map/ppermute | solution.py:25
  194.5 4.4 collective-permute-start.10
  196.4 9.2 %collective-permute-start.11 = (f32[1,8,1,16,128]{4,3,2,1,0:T(8,128)S(1)}, f32[1,8,1,16,128]{4,3,2,1,0:T(8,128)S(1)}, u32[]{:S(2)}, u32[]{:S(2)}) collective-permute-start(f32[1,8,1,16,128]{4,3,2,1,0:T(8,128)S(1)} %get-tuple-element.126), channel_id=1, source_target_pairs={{0,1},{1,2},{2,3},{3,4},{4,5},{5,6},{6,7},{7,8},{8,9},{9,10},{10,1... | collective-permute-start | bytes 196616 | tf_op jit(solution)/shard_map/ppermute | solution.py:25
  206.6 58.3 %copy-start.5 = (f32[1,8,4,16,128]{4,3,2,1,0:T(8,128)S(1)}, f32[1,8,4,16,128]{4,3,2,1,0:T(8,128)}, u32[]{:S(2)}) copy-start(f32[1,8,4,16,128]{4,3,2,1,0:T(8,128)} %get-tuple-element.23) | copy-start | bytes 786436
  206.7 160.4 %all-reduce.2.cloned.1.call-start = ((), (), s32[]{:S(2)}) async-start(), calls=%async_computation.3 | async-start | bytes 524288 | tf_op jit(solution)/shard_map/psum | solution.py:35
  265.5 9.5 %collective-permute-start.12 = (f32[1,8,1,16,128]{4,3,2,1,0:T(8,128)S(1)}, f32[1,8,1,16,128]{4,3,2,1,0:T(8,128)S(1)}, u32[]{:S(2)}, u32[]{:S(2)}) collective-permute-start(f32[1,8,1,16,128]{4,3,2,1,0:T(8,128)S(1)} %get-tuple-element.115), channel_id=1, source_target_pairs={{1,0},{2,1},{3,2},{4,3},{5,4},{6,5},{7,6},{8,7},{9,8},{10,9},{11,1... | collective-permute-start | bytes 196616 | tf_op jit(solution)/shard_map/ppermute | solution.py:28
  273.0 9.2 %collective-permute-start.13 = (f32[1,8,1,16,128]{4,3,2,1,0:T(8,128)S(1)}, f32[1,8,1,16,128]{4,3,2,1,0:T(8,128)S(1)}, u32[]{:S(2)}, u32[]{:S(2)}) collective-permute-start(f32[1,8,1,16,128]{4,3,2,1,0:T(8,128)S(1)} %get-tuple-element.116), channel_id=1, source_target_pairs={{0,1},{1,2},{2,3},{3,4},{4,5},{5,6},{6,7},{7,8},{8,9},{9,10},{10,1... | collective-permute-start | bytes 196616 | tf_op jit(solution)/shard_map/ppermute | solution.py:25
  283.3 157.7 %all-gather.13.cloned.1.call-start = ((), (), s32[]{:S(2)}) async-start(), calls=%async_computation.4 | async-start | bytes 2359296 | tf_op jit(solution)/shard_map/all_gather | solution.py:136
  367.9 9.2 %collective-permute-start.14 = (f32[8,1,16,128]{3,2,1,0:T(8,128)S(1)}, f32[8,1,16,128]{3,2,1,0:T(8,128)S(1)}, u32[]{:S(2)}, u32[]{:S(2)}) collective-permute-start(f32[8,1,16,128]{3,2,1,0:T(8,128)S(1)} %get-tuple-element.103), channel_id=1, source_target_pairs={{0,1},{1,2},{2,3},{3,4},{4,5},{5,6},{6,7},{7,8},{8,9},{9,10},{10,1... | collective-permute-start | bytes 196616 | tf_op jit(solution)/shard_map/ppermute | solution.py:25
  369.8 9.1 %collective-permute-start.15 = (f32[8,1,16,128]{3,2,1,0:T(8,128)S(1)}, f32[8,1,16,128]{3,2,1,0:T(8,128)S(1)}, u32[]{:S(2)}, u32[]{:S(2)}) collective-permute-start(f32[8,1,16,128]{3,2,1,0:T(8,128)S(1)} %get-tuple-element.104), channel_id=1, source_target_pairs={{1,0},{2,1},{3,2},{4,3},{5,4},{6,5},{7,6},{8,7},{9,8},{10,9},{11,1... | collective-permute-start | bytes 196616 | tf_op jit(solution)/shard_map/ppermute | solution.py:28
  380.2 1.2 copy-start
  381.4 148.3 %all-gather.15.cloned.1.call-start = ((), (), s32[]{:S(2)}) async-start(), calls=%async_computation.5 | async-start | bytes 2359296 | tf_op jit(solution)/shard_map/all_gather | solution.py:136
  381.5 64.0 %collective-permute-start.16 = (f32[1,8,1,16,128]{4,3,2,1,0:T(8,128)S(1)}, f32[1,8,1,16,128]{4,3,2,1,0:T(8,128)S(1)}, u32[]{:S(2)}, u32[]{:S(2)}) collective-permute-start(f32[1,8,1,16,128]{4,3,2,1,0:T(8,128)S(1)} %get-tuple-element.105), channel_id=1, source_target_pairs={{1,0},{2,1},{3,2},{4,3},{5,4},{6,5},{7,6},{8,7},{9,8},{10,9},{11,1... | collective-permute-start | bytes 196616 | tf_op jit(solution)/shard_map/ppermute | solution.py:28
  388.8 56.7 %collective-permute-start.17 = (f32[1,8,1,16,128]{4,3,2,1,0:T(8,128)S(1)}, f32[1,8,1,16,128]{4,3,2,1,0:T(8,128)S(1)}, u32[]{:S(2)}, u32[]{:S(2)}) collective-permute-start(f32[1,8,1,16,128]{4,3,2,1,0:T(8,128)S(1)} %get-tuple-element.106), channel_id=1, source_target_pairs={{0,1},{1,2},{2,3},{3,4},{4,5},{5,6},{6,7},{7,8},{8,9},{9,10},{10,1... | collective-permute-start | bytes 196616 | tf_op jit(solution)/shard_map/ppermute | solution.py:25
  390.8 54.6 %copy-start.6 = (f32[1,8,4,16,128]{4,3,2,1,0:T(8,128)S(1)}, f32[1,8,4,16,128]{4,3,2,1,0:T(8,128)}, u32[]{:S(2)}) copy-start(f32[1,8,4,16,128]{4,3,2,1,0:T(8,128)} %fusion.53) | copy-start | bytes 786436
  446.2 9.5 %collective-permute-start.18 = (f32[1,8,1,16,128]{4,3,2,1,0:T(8,128)S(1)}, f32[1,8,1,16,128]{4,3,2,1,0:T(8,128)S(1)}, u32[]{:S(2)}, u32[]{:S(2)}) collective-permute-start(f32[1,8,1,16,128]{4,3,2,1,0:T(8,128)S(1)} %get-tuple-element.93), channel_id=1, source_target_pairs={{1,0},{2,1},{3,2},{4,3},{5,4},{6,5},{7,6},{8,7},{9,8},{10,9},{11,1... | collective-permute-start | bytes 196616 | tf_op jit(solution)/shard_map/ppermute | solution.py:28
  453.7 9.2 %collective-permute-start.19 = (f32[1,8,1,16,128]{4,3,2,1,0:T(8,128)S(1)}, f32[1,8,1,16,128]{4,3,2,1,0:T(8,128)S(1)}, u32[]{:S(2)}, u32[]{:S(2)}) collective-permute-start(f32[1,8,1,16,128]{4,3,2,1,0:T(8,128)S(1)} %get-tuple-element.94), channel_id=1, source_target_pairs={{0,1},{1,2},{2,3},{3,4},{4,5},{5,6},{6,7},{7,8},{8,9},{9,10},{10,1... | collective-permute-start | bytes 196616 | tf_op jit(solution)/shard_map/ppermute | solution.py:25
  463.6 4.4 collective-permute-start.20
  465.5 9.2 %collective-permute-start.21 = (f32[1,8,1,16,128]{4,3,2,1,0:T(8,128)S(1)}, f32[1,8,1,16,128]{4,3,2,1,0:T(8,128)S(1)}, u32[]{:S(2)}, u32[]{:S(2)}) collective-permute-start(f32[1,8,1,16,128]{4,3,2,1,0:T(8,128)S(1)} %get-tuple-element.84), channel_id=1, source_target_pairs={{0,1},{1,2},{2,3},{3,4},{4,5},{5,6},{6,7},{7,8},{8,9},{9,10},{10,1... | collective-permute-start | bytes 196616 | tf_op jit(solution)/shard_map/ppermute | solution.py:25
  475.7 58.3 %copy-start.4 = (f32[1,8,4,16,128]{4,3,2,1,0:T(8,128)S(1)}, f32[1,8,4,16,128]{4,3,2,1,0:T(8,128)}, u32[]{:S(2)}) copy-start(f32[1,8,4,16,128]{4,3,2,1,0:T(8,128)} %get-tuple-element.13) | copy-start | bytes 786436
  475.8 142.3 %all-gather.17.cloned.1.call-start = ((), (), s32[]{:S(2)}) async-start(), calls=%async_computation.6 | async-start | bytes 2359296 | tf_op jit(solution)/shard_map/all_gather | solution.py:136
  534.6 9.5 %collective-permute-start.22 = (f32[1,8,1,16,128]{4,3,2,1,0:T(8,128)S(1)}, f32[1,8,1,16,128]{4,3,2,1,0:T(8,128)S(1)}, u32[]{:S(2)}, u32[]{:S(2)}) collective-permute-start(f32[1,8,1,16,128]{4,3,2,1,0:T(8,128)S(1)} %get-tuple-element.73), channel_id=1, source_target_pairs={{1,0},{2,1},{3,2},{4,3},{5,4},{6,5},{7,6},{8,7},{9,8},{10,9},{11,1... | collective-permute-start | bytes 196616 | tf_op jit(solution)/shard_map/ppermute | solution.py:28
  542.1 9.2 %collective-permute-start.23 = (f32[1,8,1,16,128]{4,3,2,1,0:T(8,128)S(1)}, f32[1,8,1,16,128]{4,3,2,1,0:T(8,128)S(1)}, u32[]{:S(2)}, u32[]{:S(2)}) collective-permute-start(f32[1,8,1,16,128]{4,3,2,1,0:T(8,128)S(1)} %get-tuple-element.74), channel_id=1, source_target_pairs={{0,1},{1,2},{2,3},{3,4},{4,5},{5,6},{6,7},{7,8},{8,9},{9,10},{10,1... | collective-permute-start | bytes 196616 | tf_op jit(solution)/shard_map/ppermute | solution.py:25
  552.1 4.4 collective-permute-start.24
  554.0 9.2 %collective-permute-start.25 = (f32[1,8,1,16,128]{4,3,2,1,0:T(8,128)S(1)}, f32[1,8,1,16,128]{4,3,2,1,0:T(8,128)S(1)}, u32[]{:S(2)}, u32[]{:S(2)}) collective-permute-start(f32[1,8,1,16,128]{4,3,2,1,0:T(8,128)S(1)} %get-tuple-element.64), channel_id=1, source_target_pairs={{0,1},{1,2},{2,3},{3,4},{4,5},{5,6},{6,7},{7,8},{8,9},{9,10},{10,1... | collective-permute-start | bytes 196616 | tf_op jit(solution)/shard_map/ppermute | solution.py:25
  564.2 58.3 %copy-start.3 = (f32[1,8,4,16,128]{4,3,2,1,0:T(8,128)S(1)}, f32[1,8,4,16,128]{4,3,2,1,0:T(8,128)}, u32[]{:S(2)}) copy-start(f32[1,8,4,16,128]{4,3,2,1,0:T(8,128)} %get-tuple-element.7) | copy-start | bytes 786436
  623.1 9.5 %collective-permute-start.26 = (f32[1,8,1,16,128]{4,3,2,1,0:T(8,128)S(1)}, f32[1,8,1,16,128]{4,3,2,1,0:T(8,128)S(1)}, u32[]{:S(2)}, u32[]{:S(2)}) collective-permute-start(f32[1,8,1,16,128]{4,3,2,1,0:T(8,128)S(1)} %get-tuple-element.61), channel_id=1, source_target_pairs={{1,0},{2,1},{3,2},{4,3},{5,4},{6,5},{7,6},{8,7},{9,8},{10,9},{11,1... | collective-permute-start | bytes 196616 | tf_op jit(solution)/shard_map/ppermute | solution.py:28
  630.6 9.2 %collective-permute-start.27 = (f32[1,8,1,16,128]{4,3,2,1,0:T(8,128)S(1)}, f32[1,8,1,16,128]{4,3,2,1,0:T(8,128)S(1)}, u32[]{:S(2)}, u32[]{:S(2)}) collective-permute-start(f32[1,8,1,16,128]{4,3,2,1,0:T(8,128)S(1)} %get-tuple-element.62), channel_id=1, source_target_pairs={{0,1},{1,2},{2,3},{3,4},{4,5},{5,6},{6,7},{7,8},{8,9},{9,10},{10,1... | collective-permute-start | bytes 196616 | tf_op jit(solution)/shard_map/ppermute | solution.py:25
Sparse Core Ops, SparseCore 0:
  27.6 55.7 all-gather.6
  118.3 53.7 all-gather.8
  206.8 53.7 all-gather.10
  283.5 83.5 all-reduce.1
  381.5 59.4 all-gather.12
  475.9 53.7 all-gather.14
  564.3 53.7 all-gather.16
where the time goes:
time: 649 us; the launch traced here: 648 us
  waiting for transfers between devices  469 us (72%)
  starting transfers between devices  116 us (18%)
  matrix products  26.6 us (4%)
  between operations  16 us (2%)
  other arithmetic  13.8 us (2%)
  local copies, waits for them, and re-layouts  6.91 us (1%)
    all_gather x6, waiting for transfers between devices, on_device(): piece = lax.all_gather(rates, 'node', axis=0, tiled=True)  313 us
    ppermute x14, starting transfers between devices, with_halo(): lax.ppermute(lax.slice_in_dim(block, 0, width, axis=dim), axis, backward)  86.3 us
    psum x1, waiting for transfers between devices, broadcast(): return lax.psum(block, axis)  83.6 us
    ppermute x14, waiting for transfers between devices, with_halo(): lax.ppermute(lax.slice_in_dim(block, block.shape[dim] - width, None, axis...  70.3 us
    ppermute x14, starting transfers between devices, with_halo(): lax.ppermute(lax.slice_in_dim(block, block.shape[dim] - width, None, axis...  28.8 us
    dot_general x6, matrix products, on_device(): jnp.tensordot(coefs, piece, axes=1, precision=lax.Precision.HIGHEST)  26.6 us
  transfers between devices with their start and end apart: 35, of which 18 were waited for; matrix products, arithmetic and copies ran while one was open for 2% of the time, Pallas kernels for 0%

commit v1 on v0

--- a/solution.py
+++ b/solution.py
@@ -32,7 +32,7 @@
 
 def broadcast(block, axis, source):
     block = jnp.where(lax.axis_index(axis) == source, block, jnp.zeros_like(block))
-    return lax.psum(block, axis)
+    return jnp.sum(lax.all_gather(block, axis), axis=0)
 
 
 def legendre_pair(count, point):

time: 649 us -> 620 us (0.955)
  waiting for transfers between devices: 469 us -> 439 us
    psum x1 -> x0, waiting for transfers between devices: 83.6 us -> none  [broadcast(): return lax.psum(block, axis)]
    all_gather x0 -> x1, waiting for transfers between devices: none -> 53.8 us  [broadcast(): return jnp.sum(lax.all_gather(block, axis), axis=0)]
where the time goes in v1:
time: 620 us; the launch traced here: 618 us
  waiting for transfers between devices  439 us (71%)
  starting transfers between devices  116 us (19%)
  matrix products  26.6 us (4%)
  between operations  16 us (3%)
  other arithmetic  14.6 us (2%)
    all_gather x6, waiting for transfers between devices, on_device(): piece = lax.all_gather(rates, 'node', axis=0, tiled=True)  313 us
    ppermute x14, starting transfers between devices, with_halo(): lax.ppermute(lax.slice_in_dim(block, 0, width, axis=dim), axis, backward)  86.6 us
    ppermute x14, waiting for transfers between devices, with_halo(): lax.ppermute(lax.slice_in_dim(block, block.shape[dim] - width, None, axis...  70.3 us
    all_gather x1, waiting for transfers between devices, broadcast(): return jnp.sum(lax.all_gather(block, axis), axis=0)  53.8 us
    ppermute x14, starting transfers between devices, with_halo(): lax.ppermute(lax.slice_in_dim(block, block.shape[dim] - width, None, axis...  28.8 us
    dot_general x6, matrix products, on_device(): jnp.tensordot(coefs, piece, axes=1, precision=lax.Precision.HIGHEST)  26.6 us
  transfers between devices with their start and end apart: 35, of which 18 were waited for; matrix products, arithmetic and copies ran while one was open for 2% of the time, Pallas kernels for 0%

profile of v1, /device:TPU:8, one launch (start us, length us, event | category | flops | bytes accessed | tf_op | source)
XLA Modules:
  0.0 618.4 jit_solution(1358860211013787253)
XLA Ops:
  7.3 1.9 collective-permute-start
  9.3 13.3 %collective-permute-start.1 = (f32[8,1,16,128]{3,2,1,0:T(8,128)S(1)}, f32[8,1,16,128]{3,2,1,0:T(8,128)S(1)}, u32[]{:S(2)}, u32[]{:S(2)}) collective-permute-start(f32[8,1,16,128]{3,2,1,0:T(8,128)S(1)} %get-tuple-element.167), channel_id=1, source_target_pairs={{1,0},{2,1},{3,2},{4,3},{5,4},{6,5},{7,6},{8,7},{9,8},{10,9},{11,1... | collective-permute-start | bytes 196616 | tf_op jit(solution)/shard_map/ppermute | solution.py:28
  27.6 5.7 collective-permute-start.2
  33.3 1.9 collective-permute-start.3
  35.7 47.7 %all-gather.8.cloned.1.call-done = f32[8,8,4,16,128]{4,3,2,1,0:T(8,128)} async-done(((f32[1,8,4,16,128]{4,3,2,1,0:T(8,128)}), f32[8,8,4,16,128]{4,3,2,1,0:T(8,128)}) %all-gather.8.cloned.1.call-update) | async-done | bytes 2097168 | tf_op jit(solution)/shard_map/all_gather | solution.py:136
  83.4 4.4 fusion.10
  88.6 7.5 %collective-permute-start.4 = (f32[1,8,1,16,128]{4,3,2,1,0:T(8,128)S(1)}, f32[1,8,1,16,128]{4,3,2,1,0:T(8,128)S(1)}, u32[]{:S(2)}, u32[]{:S(2)}) collective-permute-start(f32[1,8,1,16,128]{4,3,2,1,0:T(8,128)S(1)} %get-tuple-element.156), channel_id=1, source_target_pairs={{1,0},{2,1},{3,2},{4,3},{5,4},{6,5},{7,6},{8,7},{9,8},{10,9},{11,1... | collective-permute-start | bytes 196616 | tf_op jit(solution)/shard_map/ppermute | solution.py:28
  96.1 1.9 collective-permute-start.5
  98.1 7.2 %collective-permute-done.5 = f32[1,8,1,16,128]{4,3,2,1,0:T(8,128)S(1)} collective-permute-done((f32[1,8,1,16,128]{4,3,2,1,0:T(8,128)S(1)}, f32[1,8,1,16,128]{4,3,2,1,0:T(8,128)S(1)}, u32[]{:S(2)}, u32[]{:S(2)}) %collective-permute-start.5) | collective-permute-done | bytes 65568 | tf_op jit(solution)/shard_map/ppermute | solution.py:25
  106.0 1.9 collective-permute-start.6
  108.0 2.4 collective-permute-start.7
  110.4 6.7 %collective-permute-done.7 = f32[1,8,1,16,128]{4,3,2,1,0:T(8,128)S(1)} collective-permute-done((f32[1,8,1,16,128]{4,3,2,1,0:T(8,128)S(1)}, f32[1,8,1,16,128]{4,3,2,1,0:T(8,128)S(1)}, u32[]{:S(2)}, u32[]{:S(2)}) %collective-permute-start.7) | collective-permute-done | bytes 65568 | tf_op jit(solution)/shard_map/ppermute | solution.py:25
  118.2 53.8 %all-gather.10.cloned.1.call-done = f32[8,8,4,16,128]{4,3,2,1,0:T(8,128)} async-done(((f32[1,8,4,16,128]{4,3,2,1,0:T(8,128)}), f32[8,8,4,16,128]{4,3,2,1,0:T(8,128)}) %all-gather.10.cloned.1.call-update) | async-done | bytes 2097168 | tf_op jit(solution)/shard_map/all_gather | solution.py:136
  172.1 4.4 fusion.8
  177.1 7.5 %collective-permute-start.8 = (f32[1,8,1,16,128]{4,3,2,1,0:T(8,128)S(1)}, f32[1,8,1,16,128]{4,3,2,1,0:T(8,128)S(1)}, u32[]{:S(2)}, u32[]{:S(2)}) collective-permute-start(f32[1,8,1,16,128]{4,3,2,1,0:T(8,128)S(1)} %get-tuple-element.136), channel_id=1, source_target_pairs={{1,0},{2,1},{3,2},{4,3},{5,4},{6,5},{7,6},{8,7},{9,8},{10,9},{11,1... | collective-permute-start | bytes 196616 | tf_op jit(solution)/shard_map/ppermute | solution.py:28
  184.6 1.9 collective-permute-start.9
  186.5 7.2 %collective-permute-done.9 = f32[1,8,1,16,128]{4,3,2,1,0:T(8,128)S(1)} collective-permute-done((f32[1,8,1,16,128]{4,3,2,1,0:T(8,128)S(1)}, f32[1,8,1,16,128]{4,3,2,1,0:T(8,128)S(1)}, u32[]{:S(2)}, u32[]{:S(2)}) %collective-permute-start.9) | collective-permute-done | bytes 65568 | tf_op jit(solution)/shard_map/ppermute | solution.py:25
  194.5 1.9 collective-permute-start.10
  196.4 2.4 collective-permute-start.11
  198.9 6.7 %collective-permute-done.11 = f32[1,8,1,16,128]{4,3,2,1,0:T(8,128)S(1)} collective-permute-done((f32[1,8,1,16,128]{4,3,2,1,0:T(8,128)S(1)}, f32[1,8,1,16,128]{4,3,2,1,0:T(8,128)S(1)}, u32[]{:S(2)}, u32[]{:S(2)}) %collective-permute-start.11) | collective-permute-done | bytes 65568 | tf_op jit(solution)/shard_map/ppermute | solution.py:25
  206.9 53.6 %all-gather.12.cloned.1.call-done = f32[8,8,4,16,128]{4,3,2,1,0:T(8,128)} async-done(((f32[1,8,4,16,128]{4,3,2,1,0:T(8,128)}), f32[8,8,4,16,128]{4,3,2,1,0:T(8,128)}) %all-gather.12.cloned.1.call-update) | async-done | bytes 2097168 | tf_op jit(solution)/shard_map/all_gather | solution.py:136
  260.5 4.4 fusion.6
  265.5 7.5 %collective-permute-start.12 = (f32[1,8,1,16,128]{4,3,2,1,0:T(8,128)S(1)}, f32[1,8,1,16,128]{4,3,2,1,0:T(8,128)S(1)}, u32[]{:S(2)}, u32[]{:S(2)}) collective-permute-start(f32[1,8,1,16,128]{4,3,2,1,0:T(8,128)S(1)} %get-tuple-element.116), channel_id=1, source_target_pairs={{1,0},{2,1},{3,2},{4,3},{5,4},{6,5},{7,6},{8,7},{9,8},{10,9},{11,1... | collective-permute-start | bytes 196616 | tf_op jit(solution)/shard_map/ppermute | solution.py:28
  273.0 1.9 collective-permute-start.13
  275.0 7.2 %collective-permute-done.13 = f32[1,8,1,16,128]{4,3,2,1,0:T(8,128)S(1)} collective-permute-done((f32[1,8,1,16,128]{4,3,2,1,0:T(8,128)S(1)}, f32[1,8,1,16,128]{4,3,2,1,0:T(8,128)S(1)}, u32[]{:S(2)}, u32[]{:S(2)}) %collective-permute-start.13) | collective-permute-done | bytes 65568 | tf_op jit(solution)/shard_map/ppermute | solution.py:25
  283.4 53.8 %all-gather.14.cloned.1.call-done = f32[8,8,4,16,128]{4,3,2,1,0:T(8,128)} async-done(((f32[1,8,4,16,128]{4,3,2,1,0:T(8,128)}), f32[8,8,4,16,128]{4,3,2,1,0:T(8,128)}) %all-gather.14.cloned.1.call-update) | async-done | bytes 2097168 | tf_op jit(solution)/shard_map/all_gather | solution.py:35
  339.0 1.9 collective-permute-start.14
  340.9 7.5 %collective-permute-start.15 = (f32[8,1,16,128]{3,2,1,0:T(8,128)S(1)}, f32[8,1,16,128]{3,2,1,0:T(8,128)S(1)}, u32[]{:S(2)}, u32[]{:S(2)}) collective-permute-start(f32[8,1,16,128]{3,2,1,0:T(8,128)S(1)} %get-tuple-element.105), channel_id=1, source_target_pairs={{1,0},{2,1},{3,2},{4,3},{5,4},{6,5},{7,6},{8,7},{9,8},{10,9},{11,1... | collective-permute-start | bytes 196616 | tf_op jit(solution)/shard_map/ppermute | solution.py:28
  351.8 7.3 %collective-permute-start.16 = (f32[1,8,1,16,128]{4,3,2,1,0:T(8,128)S(1)}, f32[1,8,1,16,128]{4,3,2,1,0:T(8,128)S(1)}, u32[]{:S(2)}, u32[]{:S(2)}) collective-permute-start(f32[1,8,1,16,128]{4,3,2,1,0:T(8,128)S(1)} %get-tuple-element.106), channel_id=1, source_target_pairs={{1,0},{2,1},{3,2},{4,3},{5,4},{6,5},{7,6},{8,7},{9,8},{10,9},{11,1... | collective-permute-start | bytes 196616 | tf_op jit(solution)/shard_map/ppermute | solution.py:28
  359.1 1.9 collective-permute-start.17
  361.5 50.3 %all-gather.16.cloned.1.call-done = f32[8,8,4,16,128]{4,3,2,1,0:T(8,128)} async-done(((f32[1,8,4,16,128]{4,3,2,1,0:T(8,128)}), f32[8,8,4,16,128]{4,3,2,1,0:T(8,128)}) %all-gather.16.cloned.1.call-update) | async-done | bytes 2097168 | tf_op jit(solution)/shard_map/all_gather | solution.py:136
  411.7 4.4 fusion.4
  416.9 7.5 %collective-permute-start.18 = (f32[1,8,1,16,128]{4,3,2,1,0:T(8,128)S(1)}, f32[1,8,1,16,128]{4,3,2,1,0:T(8,128)S(1)}, u32[]{:S(2)}, u32[]{:S(2)}) collective-permute-start(f32[1,8,1,16,128]{4,3,2,1,0:T(8,128)S(1)} %get-tuple-element.94), channel_id=1, source_target_pairs={{1,0},{2,1},{3,2},{4,3},{5,4},{6,5},{7,6},{8,7},{9,8},{10,9},{11,1... | collective-permute-start | bytes 196616 | tf_op jit(solution)/shard_map/ppermute | solution.py:28
  424.4 1.9 collective-permute-start.19
  426.4 7.2 %collective-permute-done.19 = f32[1,8,1,16,128]{4,3,2,1,0:T(8,128)S(1)} collective-permute-done((f32[1,8,1,16,128]{4,3,2,1,0:T(8,128)S(1)}, f32[1,8,1,16,128]{4,3,2,1,0:T(8,128)S(1)}, u32[]{:S(2)}, u32[]{:S(2)}) %collective-permute-start.19) | collective-permute-done | bytes 65568 | tf_op jit(solution)/shard_map/ppermute | solution.py:25
  434.3 1.9 collective-permute-start.20
  436.2 2.4 collective-permute-start.21
  438.7 6.7 %collective-permute-done.21 = f32[1,8,1,16,128]{4,3,2,1,0:T(8,128)S(1)} collective-permute-done((f32[1,8,1,16,128]{4,3,2,1,0:T(8,128)S(1)}, f32[1,8,1,16,128]{4,3,2,1,0:T(8,128)S(1)}, u32[]{:S(2)}, u32[]{:S(2)}) %collective-permute-start.21) | collective-permute-done | bytes 65568 | tf_op jit(solution)/shard_map/ppermute | solution.py:25
  446.7 53.6 %all-gather.18.cloned.1.call-done = f32[8,8,4,16,128]{4,3,2,1,0:T(8,128)} async-done(((f32[1,8,4,16,128]{4,3,2,1,0:T(8,128)}), f32[8,8,4,16,128]{4,3,2,1,0:T(8,128)}) %all-gather.18.cloned.1.call-update) | async-done | bytes 2097168 | tf_op jit(solution)/shard_map/all_gather | solution.py:136
  500.3 4.4 fusion.2
  505.3 7.5 %collective-permute-start.22 = (f32[1,8,1,16,128]{4,3,2,1,0:T(8,128)S(1)}, f32[1,8,1,16,128]{4,3,2,1,0:T(8,128)S(1)}, u32[]{:S(2)}, u32[]{:S(2)}) collective-permute-start(f32[1,8,1,16,128]{4,3,2,1,0:T(8,128)S(1)} %get-tuple-element.74), channel_id=1, source_target_pairs={{1,0},{2,1},{3,2},{4,3},{5,4},{6,5},{7,6},{8,7},{9,8},{10,9},{11,1... | collective-permute-start | bytes 196616 | tf_op jit(solution)/shard_map/ppermute | solution.py:28
  514.8 7.2 %collective-permute-done.23 = f32[1,8,1,16,128]{4,3,2,1,0:T(8,128)S(1)} collective-permute-done((f32[1,8,1,16,128]{4,3,2,1,0:T(8,128)S(1)}, f32[1,8,1,16,128]{4,3,2,1,0:T(8,128)S(1)}, u32[]{:S(2)}, u32[]{:S(2)}) %collective-permute-start.23) | collective-permute-done | bytes 65568 | tf_op jit(solution)/shard_map/ppermute | solution.py:25
  524.7 2.4 collective-permute-start.25
  527.1 6.7 %collective-permute-done.25 = f32[1,8,1,16,128]{4,3,2,1,0:T(8,128)S(1)} collective-permute-done((f32[1,8,1,16,128]{4,3,2,1,0:T(8,128)S(1)}, f32[1,8,1,16,128]{4,3,2,1,0:T(8,128)S(1)}, u32[]{:S(2)}, u32[]{:S(2)}) %collective-permute-start.25) | collective-permute-done | bytes 65568 | tf_op jit(solution)/shard_map/ppermute | solution.py:25
  534.9 53.9 %all-gather.20.cloned.1.call-done = f32[8,8,4,16,128]{4,3,2,1,0:T(8,128)} async-done(((f32[1,8,4,16,128]{4,3,2,1,0:T(8,128)}), f32[8,8,4,16,128]{4,3,2,1,0:T(8,128)}) %all-gather.20.cloned.1.call-update) | async-done | bytes 2097168 | tf_op jit(solution)/shard_map/all_gather | solution.py:136
  588.8 4.4 fusion
  593.8 7.5 %collective-permute-start.26 = (f32[1,8,1,16,128]{4,3,2,1,0:T(8,128)S(1)}, f32[1,8,1,16,128]{4,3,2,1,0:T(8,128)S(1)}, u32[]{:S(2)}, u32[]{:S(2)}) collective-permute-start(f32[1,8,1,16,128]{4,3,2,1,0:T(8,128)S(1)} %get-tuple-element.62), channel_id=1, source_target_pairs={{1,0},{2,1},{3,2},{4,3},{5,4},{6,5},{7,6},{8,7},{9,8},{10,9},{11,1... | collective-permute-start | bytes 196616 | tf_op jit(solution)/shard_map/ppermute | solution.py:28
  603.2 7.2 %collective-permute-done.27 = f32[1,8,1,16,128]{4,3,2,1,0:T(8,128)S(1)} collective-permute-done((f32[1,8,1,16,128]{4,3,2,1,0:T(8,128)S(1)}, f32[1,8,1,16,128]{4,3,2,1,0:T(8,128)S(1)}, u32[]{:S(2)}, u32[]{:S(2)}) %collective-permute-start.27) | collective-permute-done | bytes 65568 | tf_op jit(solution)/shard_map/ppermute | solution.py:25
  (150 shorter events, 29.0 us)
Async XLA Ops:
  6.5 76.9 %all-gather.8.cloned.1.call-start = ((), (), s32[]{:S(2)}) async-start(), calls=%async_computation | async-start | bytes 2359296 | tf_op jit(solution)/shard_map/all_gather | solution.py:136
  7.3 18.7 %collective-permute-start = (f32[8,1,16,128]{3,2,1,0:T(8,128)S(1)}, f32[8,1,16,128]{3,2,1,0:T(8,128)S(1)}, u32[]{:S(2)}, u32[]{:S(2)}) collective-permute-start(f32[8,1,16,128]{3,2,1,0:T(8,128)S(1)} %get-tuple-element.166), channel_id=1, source_target_pairs={{0,1},{1,2},{2,3},{3,4},{4,5},{5,6},{6,7},{7,8},{8,9},{9,10},{10,1... | collective-permute-start | bytes 196616 | tf_op jit(solution)/shard_map/ppermute | solution.py:25
  9.3 16.8 %collective-permute-start.1 = (f32[8,1,16,128]{3,2,1,0:T(8,128)S(1)}, f32[8,1,16,128]{3,2,1,0:T(8,128)S(1)}, u32[]{:S(2)}, u32[]{:S(2)}) collective-permute-start(f32[8,1,16,128]{3,2,1,0:T(8,128)S(1)} %get-tuple-element.167), channel_id=1, source_target_pairs={{1,0},{2,1},{3,2},{4,3},{5,4},{6,5},{7,6},{8,7},{9,8},{10,9},{11,1... | collective-permute-start | bytes 196616 | tf_op jit(solution)/shard_map/ppermute | solution.py:28
  26.3 1.2 copy-start.5
  27.5 55.9 %copy-start.7 = (f32[8,8]{1,0:T(8,128)S(1)}, f32[8,8]{1,0:T(8,128)}, u32[]{:S(2)}) copy-start(f32[8,8]{1,0:T(8,128)} %constant.57.clone) | copy-start | bytes 772
  27.5 144.6 %all-gather.10.cloned.1.call-start = ((), (), s32[]{:S(2)}) async-start(), calls=%async_computation.1 | async-start | bytes 2359296 | tf_op jit(solution)/shard_map/all_gather | solution.py:136
  27.6 60.3 %collective-permute-start.2 = (f32[1,8,1,16,128]{4,3,2,1,0:T(8,128)S(1)}, f32[1,8,1,16,128]{4,3,2,1,0:T(8,128)S(1)}, u32[]{:S(2)}, u32[]{:S(2)}) collective-permute-start(f32[1,8,1,16,128]{4,3,2,1,0:T(8,128)S(1)} %get-tuple-element.168), channel_id=1, source_target_pairs={{1,0},{2,1},{3,2},{4,3},{5,4},{6,5},{7,6},{8,7},{9,8},{10,9},{11,1... | collective-permute-start | bytes 196616 | tf_op jit(solution)/shard_map/ppermute | solution.py:28
  33.3 54.5 %collective-permute-start.3 = (f32[1,8,1,16,128]{4,3,2,1,0:T(8,128)S(1)}, f32[1,8,1,16,128]{4,3,2,1,0:T(8,128)S(1)}, u32[]{:S(2)}, u32[]{:S(2)}) collective-permute-start(f32[1,8,1,16,128]{4,3,2,1,0:T(8,128)S(1)} %get-tuple-element.169), channel_id=1, source_target_pairs={{0,1},{1,2},{2,3},{3,4},{4,5},{5,6},{6,7},{7,8},{8,9},{9,10},{10,1... | collective-permute-start | bytes 196616 | tf_op jit(solution)/shard_map/ppermute | solution.py:25
  35.4 52.5 %copy-start.1 = (f32[1,8,4,16,128]{4,3,2,1,0:T(8,128)S(1)}, f32[1,8,4,16,128]{4,3,2,1,0:T(8,128)}, u32[]{:S(2)}) copy-start(f32[1,8,4,16,128]{4,3,2,1,0:T(8,128)} %fusion.21) | copy-start | bytes 786436
  88.6 9.5 %collective-permute-start.4 = (f32[1,8,1,16,128]{4,3,2,1,0:T(8,128)S(1)}, f32[1,8,1,16,128]{4,3,2,1,0:T(8,128)S(1)}, u32[]{:S(2)}, u32[]{:S(2)}) collective-permute-start(f32[1,8,1,16,128]{4,3,2,1,0:T(8,128)S(1)} %get-tuple-element.156), channel_id=1, source_target_pairs={{1,0},{2,1},{3,2},{4,3},{5,4},{6,5},{7,6},{8,7},{9,8},{10,9},{11,1... | collective-permute-start | bytes 196616 | tf_op jit(solution)/shard_map/ppermute | solution.py:28
  96.1 9.2 %collective-permute-start.5 = (f32[1,8,1,16,128]{4,3,2,1,0:T(8,128)S(1)}, f32[1,8,1,16,128]{4,3,2,1,0:T(8,128)S(1)}, u32[]{:S(2)}, u32[]{:S(2)}) collective-permute-start(f32[1,8,1,16,128]{4,3,2,1,0:T(8,128)S(1)} %get-tuple-element.157), channel_id=1, source_target_pairs={{0,1},{1,2},{2,3},{3,4},{4,5},{5,6},{6,7},{7,8},{8,9},{9,10},{10,1... | collective-permute-start | bytes 196616 | tf_op jit(solution)/shard_map/ppermute | solution.py:25
  106.0 4.4 collective-permute-start.6
  108.0 9.2 %collective-permute-start.7 = (f32[1,8,1,16,128]{4,3,2,1,0:T(8,128)S(1)}, f32[1,8,1,16,128]{4,3,2,1,0:T(8,128)S(1)}, u32[]{:S(2)}, u32[]{:S(2)}) collective-permute-start(f32[1,8,1,16,128]{4,3,2,1,0:T(8,128)S(1)} %get-tuple-element.147), channel_id=1, source_target_pairs={{0,1},{1,2},{2,3},{3,4},{4,5},{5,6},{6,7},{7,8},{8,9},{9,10},{10,1... | collective-permute-start | bytes 196616 | tf_op jit(solution)/shard_map/ppermute | solution.py:25
  118.2 58.3 %copy-start = (f32[1,8,4,16,128]{4,3,2,1,0:T(8,128)S(1)}, f32[1,8,4,16,128]{4,3,2,1,0:T(8,128)}, u32[]{:S(2)}) copy-start(f32[1,8,4,16,128]{4,3,2,1,0:T(8,128)} %get-tuple-element.30) | copy-start | bytes 786436
  118.2 142.3 %all-gather.12.cloned.1.call-start = ((), (), s32[]{:S(2)}) async-start(), calls=%async_computation.2 | async-start | bytes 2359296 | tf_op jit(solution)/shard_map/all_gather | solution.py:136
  177.1 9.5 %collective-permute-start.8 = (f32[1,8,1,16,128]{4,3,2,1,0:T(8,128)S(1)}, f32[1,8,1,16,128]{4,3,2,1,0:T(8,128)S(1)}, u32[]{:S(2)}, u32[]{:S(2)}) collective-permute-start(f32[1,8,1,16,128]{4,3,2,1,0:T(8,128)S(1)} %get-tuple-element.136), channel_id=1, source_target_pairs={{1,0},{2,1},{3,2},{4,3},{5,4},{6,5},{7,6},{8,7},{9,8},{10,9},{11,1... | collective-permute-start | bytes 196616 | tf_op jit(solution)/shard_map/ppermute | solution.py:28
  184.6 9.2 %collective-permute-start.9 = (f32[1,8,1,16,128]{4,3,2,1,0:T(8,128)S(1)}, f32[1,8,1,16,128]{4,3,2,1,0:T(8,128)S(1)}, u32[]{:S(2)}, u32[]{:S(2)}) collective-permute-start(f32[1,8,1,16,128]{4,3,2,1,0:T(8,128)S(1)} %get-tuple-element.137), channel_id=1, source_target_pairs={{0,1},{1,2},{2,3},{3,4},{4,5},{5,6},{6,7},{7,8},{8,9},{9,10},{10,1... | collective-permute-start | bytes 196616 | tf_op jit(solution)/shard_map/ppermute | solution.py:25
  194.5 4.4 collective-permute-start.10
  196.4 9.2 %collective-permute-start.11 = (f32[1,8,1,16,128]{4,3,2,1,0:T(8,128)S(1)}, f32[1,8,1,16,128]{4,3,2,1,0:T(8,128)S(1)}, u32[]{:S(2)}, u32[]{:S(2)}) collective-permute-start(f32[1,8,1,16,128]{4,3,2,1,0:T(8,128)S(1)} %get-tuple-element.127), channel_id=1, source_target_pairs={{0,1},{1,2},{2,3},{3,4},{4,5},{5,6},{6,7},{7,8},{8,9},{9,10},{10,1... | collective-permute-start | bytes 196616 | tf_op jit(solution)/shard_map/ppermute | solution.py:25
  206.6 58.3 %copy-start.4 = (f32[1,8,4,16,128]{4,3,2,1,0:T(8,128)S(1)}, f32[1,8,4,16,128]{4,3,2,1,0:T(8,128)}, u32[]{:S(2)}) copy-start(f32[1,8,4,16,128]{4,3,2,1,0:T(8,128)} %get-tuple-element.24) | copy-start | bytes 786436
  206.7 130.5 %all-gather.14.cloned.1.call-start = ((), (), s32[]{:S(2)}) async-start(), calls=%async_computation.3 | async-start | bytes 2359296 | tf_op jit(solution)/shard_map/all_gather | solution.py:35
  265.5 9.5 %collective-permute-start.12 = (f32[1,8,1,16,128]{4,3,2,1,0:T(8,128)S(1)}, f32[1,8,1,16,128]{4,3,2,1,0:T(8,128)S(1)}, u32[]{:S(2)}, u32[]{:S(2)}) collective-permute-start(f32[1,8,1,16,128]{4,3,2,1,0:T(8,128)S(1)} %get-tuple-element.116), channel_id=1, source_target_pairs={{1,0},{2,1},{3,2},{4,3},{5,4},{6,5},{7,6},{8,7},{9,8},{10,9},{11,1... | collective-permute-start | bytes 196616 | tf_op jit(solution)/shard_map/ppermute | solution.py:28
  273.0 9.2 %collective-permute-start.13 = (f32[1,8,1,16,128]{4,3,2,1,0:T(8,128)S(1)}, f32[1,8,1,16,128]{4,3,2,1,0:T(8,128)S(1)}, u32[]{:S(2)}, u32[]{:S(2)}) collective-permute-start(f32[1,8,1,16,128]{4,3,2,1,0:T(8,128)S(1)} %get-tuple-element.117), channel_id=1, source_target_pairs={{0,1},{1,2},{2,3},{3,4},{4,5},{5,6},{6,7},{7,8},{8,9},{9,10},{10,1... | collective-permute-start | bytes 196616 | tf_op jit(solution)/shard_map/ppermute | solution.py:25
  283.3 128.4 %all-gather.16.cloned.1.call-start = ((), (), s32[]{:S(2)}) async-start(), calls=%async_computation.4 | async-start | bytes 2359296 | tf_op jit(solution)/shard_map/all_gather | solution.py:136
  339.0 9.5 %collective-permute-start.14 = (f32[8,1,16,128]{3,2,1,0:T(8,128)S(1)}, f32[8,1,16,128]{3,2,1,0:T(8,128)S(1)}, u32[]{:S(2)}, u32[]{:S(2)}) collective-permute-start(f32[8,1,16,128]{3,2,1,0:T(8,128)S(1)} %get-tuple-element.104), channel_id=1, source_target_pairs={{0,1},{1,2},{2,3},{3,4},{4,5},{5,6},{6,7},{7,8},{8,9},{9,10},{10,1... | collective-permute-start | bytes 196616 | tf_op jit(solution)/shard_map/ppermute | solution.py:25
  340.9 9.4 %collective-permute-start.15 = (f32[8,1,16,128]{3,2,1,0:T(8,128)S(1)}, f32[8,1,16,128]{3,2,1,0:T(8,128)S(1)}, u32[]{:S(2)}, u32[]{:S(2)}) collective-permute-start(f32[8,1,16,128]{3,2,1,0:T(8,128)S(1)} %get-tuple-element.105), channel_id=1, source_target_pairs={{1,0},{2,1},{3,2},{4,3},{5,4},{6,5},{7,6},{8,7},{9,8},{10,9},{11,1... | collective-permute-start | bytes 196616 | tf_op jit(solution)/shard_map/ppermute | solution.py:28
  351.8 148.6 %all-gather.18.cloned.1.call-start = ((), (), s32[]{:S(2)}) async-start(), calls=%async_computation.5 | async-start | bytes 2359296 | tf_op jit(solution)/shard_map/all_gather | solution.py:136
  351.8 64.4 %collective-permute-start.16 = (f32[1,8,1,16,128]{4,3,2,1,0:T(8,128)S(1)}, f32[1,8,1,16,128]{4,3,2,1,0:T(8,128)S(1)}, u32[]{:S(2)}, u32[]{:S(2)}) collective-permute-start(f32[1,8,1,16,128]{4,3,2,1,0:T(8,128)S(1)} %get-tuple-element.106), channel_id=1, source_target_pairs={{1,0},{2,1},{3,2},{4,3},{5,4},{6,5},{7,6},{8,7},{9,8},{10,9},{11,1... | collective-permute-start | bytes 196616 | tf_op jit(solution)/shard_map/ppermute | solution.py:28
  359.1 57.1 %collective-permute-start.17 = (f32[1,8,1,16,128]{4,3,2,1,0:T(8,128)S(1)}, f32[1,8,1,16,128]{4,3,2,1,0:T(8,128)S(1)}, u32[]{:S(2)}, u32[]{:S(2)}) collective-permute-start(f32[1,8,1,16,128]{4,3,2,1,0:T(8,128)S(1)} %get-tuple-element.107), channel_id=1, source_target_pairs={{0,1},{1,2},{2,3},{3,4},{4,5},{5,6},{6,7},{7,8},{8,9},{9,10},{10,1... | collective-permute-start | bytes 196616 | tf_op jit(solution)/shard_map/ppermute | solution.py:25
  361.2 55.0 %copy-start.6 = (f32[1,8,4,16,128]{4,3,2,1,0:T(8,128)S(1)}, f32[1,8,4,16,128]{4,3,2,1,0:T(8,128)}, u32[]{:S(2)}) copy-start(f32[1,8,4,16,128]{4,3,2,1,0:T(8,128)} %fusion.53) | copy-start | bytes 786436
  416.9 9.5 %collective-permute-start.18 = (f32[1,8,1,16,128]{4,3,2,1,0:T(8,128)S(1)}, f32[1,8,1,16,128]{4,3,2,1,0:T(8,128)S(1)}, u32[]{:S(2)}, u32[]{:S(2)}) collective-permute-start(f32[1,8,1,16,128]{4,3,2,1,0:T(8,128)S(1)} %get-tuple-element.94), channel_id=1, source_target_pairs={{1,0},{2,1},{3,2},{4,3},{5,4},{6,5},{7,6},{8,7},{9,8},{10,9},{11,1... | collective-permute-start | bytes 196616 | tf_op jit(solution)/shard_map/ppermute | solution.py:28
  424.4 9.2 %collective-permute-start.19 = (f32[1,8,1,16,128]{4,3,2,1,0:T(8,128)S(1)}, f32[1,8,1,16,128]{4,3,2,1,0:T(8,128)S(1)}, u32[]{:S(2)}, u32[]{:S(2)}) collective-permute-start(f32[1,8,1,16,128]{4,3,2,1,0:T(8,128)S(1)} %get-tuple-element.95), channel_id=1, source_target_pairs={{0,1},{1,2},{2,3},{3,4},{4,5},{5,6},{6,7},{7,8},{8,9},{9,10},{10,1... | collective-permute-start | bytes 196616 | tf_op jit(solution)/shard_map/ppermute | solution.py:25
  434.3 4.4 collective-permute-start.20
  436.2 9.2 %collective-permute-start.21 = (f32[1,8,1,16,128]{4,3,2,1,0:T(8,128)S(1)}, f32[1,8,1,16,128]{4,3,2,1,0:T(8,128)S(1)}, u32[]{:S(2)}, u32[]{:S(2)}) collective-permute-start(f32[1,8,1,16,128]{4,3,2,1,0:T(8,128)S(1)} %get-tuple-element.85), channel_id=1, source_target_pairs={{0,1},{1,2},{2,3},{3,4},{4,5},{5,6},{6,7},{7,8},{8,9},{9,10},{10,1... | collective-permute-start | bytes 196616 | tf_op jit(solution)/shard_map/ppermute | solution.py:25
  446.4 58.3 %copy-start.3 = (f32[1,8,4,16,128]{4,3,2,1,0:T(8,128)S(1)}, f32[1,8,4,16,128]{4,3,2,1,0:T(8,128)}, u32[]{:S(2)}) copy-start(f32[1,8,4,16,128]{4,3,2,1,0:T(8,128)} %get-tuple-element.13) | copy-start | bytes 786436
  446.5 142.3 %all-gather.20.cloned.1.call-start = ((), (), s32[]{:S(2)}) async-start(), calls=%async_computation.6 | async-start | bytes 2359296 | tf_op jit(solution)/shard_map/all_gather | solution.py:136
  505.3 9.5 %collective-permute-start.22 = (f32[1,8,1,16,128]{4,3,2,1,0:T(8,128)S(1)}, f32[1,8,1,16,128]{4,3,2,1,0:T(8,128)S(1)}, u32[]{:S(2)}, u32[]{:S(2)}) collective-permute-start(f32[1,8,1,16,128]{4,3,2,1,0:T(8,128)S(1)} %get-tuple-element.74), channel_id=1, source_target_pairs={{1,0},{2,1},{3,2},{4,3},{5,4},{6,5},{7,6},{8,7},{9,8},{10,9},{11,1... | collective-permute-start | bytes 196616 | tf_op jit(solution)/shard_map/ppermute | solution.py:28
  512.8 9.2 %collective-permute-start.23 = (f32[1,8,1,16,128]{4,3,2,1,0:T(8,128)S(1)}, f32[1,8,1,16,128]{4,3,2,1,0:T(8,128)S(1)}, u32[]{:S(2)}, u32[]{:S(2)}) collective-permute-start(f32[1,8,1,16,128]{4,3,2,1,0:T(8,128)S(1)} %get-tuple-element.75), channel_id=1, source_target_pairs={{0,1},{1,2},{2,3},{3,4},{4,5},{5,6},{6,7},{7,8},{8,9},{9,10},{10,1... | collective-permute-start | bytes 196616 | tf_op jit(solution)/shard_map/ppermute | solution.py:25
  522.8 4.4 collective-permute-start.24
  524.7 9.2 %collective-permute-start.25 = (f32[1,8,1,16,128]{4,3,2,1,0:T(8,128)S(1)}, f32[1,8,1,16,128]{4,3,2,1,0:T(8,128)S(1)}, u32[]{:S(2)}, u32[]{:S(2)}) collective-permute-start(f32[1,8,1,16,128]{4,3,2,1,0:T(8,128)S(1)} %get-tuple-element.65), channel_id=1, source_target_pairs={{0,1},{1,2},{2,3},{3,4},{4,5},{5,6},{6,7},{7,8},{8,9},{9,10},{10,1... | collective-permute-start | bytes 196616 | tf_op jit(solution)/shard_map/ppermute | solution.py:25
  534.9 58.3 %copy-start.2 = (f32[1,8,4,16,128]{4,3,2,1,0:T(8,128)S(1)}, f32[1,8,4,16,128]{4,3,2,1,0:T(8,128)}, u32[]{:S(2)}) copy-start(f32[1,8,4,16,128]{4,3,2,1,0:T(8,128)} %get-tuple-element.7) | copy-start | bytes 786436
  593.8 9.5 %collective-permute-start.26 = (f32[1,8,1,16,128]{4,3,2,1,0:T(8,128)S(1)}, f32[1,8,1,16,128]{4,3,2,1,0:T(8,128)S(1)}, u32[]{:S(2)}, u32[]{:S(2)}) collective-permute-start(f32[1,8,1,16,128]{4,3,2,1,0:T(8,128)S(1)} %get-tuple-element.62), channel_id=1, source_target_pairs={{1,0},{2,1},{3,2},{4,3},{5,4},{6,5},{7,6},{8,7},{9,8},{10,9},{11,1... | collective-permute-start | bytes 196616 | tf_op jit(solution)/shard_map/ppermute | solution.py:28
  601.3 9.2 %collective-permute-start.27 = (f32[1,8,1,16,128]{4,3,2,1,0:T(8,128)S(1)}, f32[1,8,1,16,128]{4,3,2,1,0:T(8,128)S(1)}, u32[]{:S(2)}, u32[]{:S(2)}) collective-permute-start(f32[1,8,1,16,128]{4,3,2,1,0:T(8,128)S(1)} %get-tuple-element.63), channel_id=1, source_target_pairs={{0,1},{1,2},{2,3},{3,4},{4,5},{5,6},{6,7},{7,8},{8,9},{9,10},{10,1... | collective-permute-start | bytes 196616 | tf_op jit(solution)/shard_map/ppermute | solution.py:25
Sparse Core Ops, SparseCore 0:
  27.6 55.7 all-gather.7
  118.3 53.7 all-gather.9
  206.8 53.7 all-gather.11
  283.5 53.7 all-gather.13
  351.9 59.8 all-gather.15
  446.6 53.7 all-gather.17
  535.0 53.7 all-gather.19
